TPU v7x, 32 devices: a whole 2x2x4 slice. The times are simulated.
32 devices in a mesh: dp: 4 (over x, core), pipe: 2 (over y), tensor: 4 (over z).
Axes of the slice: x: 2, y: 2, z: 4, core: 2. Of those that a mesh axis runs over, the one named last changes fastest.
Arguments:
- layer_input: bfloat16 [4, 2, 512, 8192], P('dp', 'pipe', None, 'tensor'), may hold values from -40 to 40
- output_grad: bfloat16 [4, 2, 512, 8192], P('dp', 'pipe', None, 'tensor'), may hold values from -6 to 6
- kv_grad: bfloat16 [4, 2, 512, 2048], P('dp', 'pipe', None, 'tensor'), may hold values from -6 to 6
- norm_gain: bfloat16 [2, 8192], P('pipe', 'tensor'), may hold values from 0.5 to 1.5
- kv_weight: bfloat16 [2, 8192, 2048], P('pipe', 'tensor'), may hold values from -0.0625 to 0.0625
Outputs:
- upstream_grad: bfloat16 [4, 2, 512, 8192], P('dp', 'pipe', None, 'tensor')
- kv_weight_grad: bfloat16 [2, 8192, 2048], P('pipe', 'tensor', 'dp')
- gain_grad: float32 [2, 8192], P('pipe', 'tensor')
All inputs are finite; a program needn't handle non-finite values.
Results may differ from a plain program's by a relative error of at most 0.009.
Values may be sent and summed in bfloat16 or wider, within the bound.
No kernel may reach another device: no remote copies, remote signals or barrier semaphores. Data moves between devices by JAX's collectives and lax.ppermute only.
A program may use at most 128 MiB of HBM per device.

v0:
```python
import jax
import jax.numpy as jnp
from jax import lax
from jax.sharding import PartitionSpec as P

D = 8192


def from_behind(block, axis, distance):
    devices = range(lax.axis_size(axis))
    route = [(i - distance, i) for i in devices if i - distance in devices]
    return lax.ppermute(block, axis, route)


def on_device(layer_input, output_grad, kv_grad, norm_gain, kv_weight):
    rows = layer_input[0, 0]
    grad_out = output_grad[0, 0]
    grad_kv = kv_grad[0, 0]
    gain_f = norm_gain[0].astype(jnp.float32)
    weight = kv_weight[0]
    values = rows.astype(jnp.float32)
    local_squares = jnp.sum(values * values, axis=1, keepdims=True)
    total_squares = lax.psum(local_squares, "tensor")
    rstd = lax.rsqrt(total_squares / D + 1e-05)
    normed = values * rstd
    hidden = (normed * gain_f).astype(jnp.bfloat16)
    piece = lax.all_gather(grad_kv, "tensor", axis=1, tiled=True)
    row_total = lax.dot_general(
        piece, weight, (((1,), (1,)), ((), ())), preferred_element_type=jnp.float32
    )
    term = lax.dot_general(
        hidden, piece, (((0,), (0,)), ((), ())), preferred_element_type=jnp.float32
    )
    weight_total = term
    wgrad = weight_total
    scaled = gain_f * row_total
    local_dot = jnp.sum(scaled * normed, axis=1, keepdims=True)
    mean_term = lax.psum(local_dot, "tensor") / D
    input_grad = (grad_out.astype(jnp.float32) + rstd * (scaled - normed * mean_term)).astype(
        jnp.bfloat16
    )
    upstream = from_behind(input_grad, "pipe", -1)
    gain_part = jnp.sum(row_total * normed, axis=0)
    gain_total = lax.psum(gain_part, "dp")
    weight_total = lax.psum_scatter(
        wgrad.astype(jnp.bfloat16), "dp", scatter_dimension=1, tiled=True
    )
    return (upstream[None, None], weight_total[None], gain_total[None])


def solution(mesh):
    in_specs = (
        P("dp", "pipe", None, "tensor"),
        P("dp", "pipe", None, "tensor"),
        P("dp", "pipe", None, "tensor"),
        P("pipe", "tensor"),
        P("pipe", "tensor", None),
    )
    out_specs = (P("dp", "pipe", None, "tensor"), P("pipe", "tensor", "dp"), P("pipe", "tensor"))
    return jax.shard_map(
        on_device, mesh=mesh, in_specs=in_specs, out_specs=out_specs, check_vma=False
    )
```

profile of v0, /device:TPU:0, one launch (start us, length us, event | category | flops | bytes accessed | tf_op | source)
XLA Modules:
  0.0 152.9 jit_solution(5806783644709270451)
XLA Ops:
  7.2 0.0 all-gather.3.cloned.1.call-start
  7.2 0.7 all-gather.3.cloned.1.call-update
  7.9 0.0 reduce-scatter.2.cloned.1.call-start
  7.9 0.7 mul.69
  8.7 2.1 %fusion.13 = f32[512]{0:T(512)S(1)} fusion(bf16[1,1,512,2048]{3,2,1,0:T(8,128)(2,1)} %param.5), kind=kLoop, calls=%fused_computation.16 | loop fusion | flops 3145216 | bytes 2099200 | tf_op jit(solution)/shard_map/reduce_sum | solution.py:22
  10.7 13.7 %psum.21 = f32[512,1]{0,1:T(1,128)S(1)} all-reduce(f32[512,1]{0,1:T(1,128)S(1)} %bitcast.37), channel_id=1, replica_groups=mesh['dp'=4,'pipe'=2,'tensor'=4] {'tensor'}, use_global_device_ids=true, to_apply=%region_1.0 | all-reduce | flops 512 | bytes 4096 | tf_op jit(solution)/shard_map/psum | solution.py:23
  24.4 33.9 %all-gather.3.cloned.1.call-done = bf16[1,1,512,2048]{3,2,1,0:T(8,128)(2,1)} async-done(((bf16[1,1,512,512]{3,2,1,0:T(8,128)(2,1)}), bf16[1,1,512,2048]{3,2,1,0:T(8,128)(2,1)}) %all-gather.3.cloned.1.call-update) | async-done | bytes 2097168 | tf_op jit(solution)/shard_map/all_gather | solution.py:27
  58.3 10.1 %convolution_convert_fusion = bf16[2048,2048]{1,0:T(8,128)(2,1)} fusion(bf16[1,1,512,2048]{3,2,1,0:T(8,128)(2,1)} %param.5, bf16[1,1,512,2048]{3,2,1,0:T(8,128)(2,1)} %all-gather.3.cloned.1.call-done, f32[2048]{0:T(1024)S(1)} %bitcast.34, f32[512]{0:T(512)S(1)} %bitcast.39), kind=kOutput, calls=%fused_computation.2 | convolution fusion | flops 4303355904 | bytes 12593152 | tf_op jit(solution)/shard_map/dot_general | solution.py:31
  68.4 0.0 copy-start
  68.4 0.0 reduce-scatter.2.cloned.1.call-update
  68.4 1.6 %copy-done = bf16[1,1,512,2048]{3,2,1,0:T(8,128)(2,1)S(1)} copy-done((bf16[1,1,512,2048]{3,2,1,0:T(8,128)(2,1)S(1)}, bf16[1,1,512,2048]{3,2,1,0:T(8,128)(2,1)}, u32[]{:S(2)}) %copy-start) | copy-done | bytes 2097176
  70.0 11.8 %fusion.12 = (f32[2048]{0:T(1024)S(1)}, f32[512]{0:T(512)S(1)}, f32[512,2048]{1,0:T(8,128)}) fusion(bf16[1,1,512,2048]{3,2,1,0:T(8,128)(2,1)S(1)} %copy-done, f32[512]{0:T(512)S(1)} %bitcast.40, f32[2048]{0:T(1024)S(1)} %bitcast.35, bf16[1,2048,2048]{2,1,0:T(8,128)(2,1)} %param.9, bf16[1,1,512,2048]{3,2,1,0:T(8,128)(2,1)} %all-gather.3.cloned.1.call-done), kind=kOutput, calls=%fused_computation.15 | convolution fusion | flops 4302304768 | bytes 16797696 | tf_op jit(solution)/shard_map/dot_general | solution.py:28
  81.8 9.0 %psum.22 = f32[512,1]{0,1:T(1,128)S(1)} all-reduce(f32[512,1]{0,1:T(1,128)S(1)} %bitcast.43), channel_id=1, replica_groups=mesh['dp'=4,'pipe'=2,'tensor'=4] {'tensor'}, use_global_device_ids=true, to_apply=%region_3.0 | all-reduce | flops 512 | bytes 4096 | tf_op jit(solution)/shard_map/psum | solution.py:38
  90.8 5.7 %fusion.10 = bf16[512,2048]{1,0:T(8,128)(2,1)} fusion(f32[512,2048]{1,0:T(8,128)} %get-tuple-element.5, bf16[1,1,512,2048]{3,2,1,0:T(8,128)(2,1)} %param.6, bf16[1,1,512,2048]{3,2,1,0:T(8,128)(2,1)S(1)} %copy-done, f32[512]{0:T(512)S(1)} %bitcast.42, f32[2048]{0:T(1024)S(1)} %bitcast.36, f32[512]{0:T(512)S(1)} %bitcast.41), kind=kLoop, calls=%fused_computation.13 | loop fusion | flops 9437184 | bytes 10498048 | tf_op jit(solution)/shard_map/convert_element_type | solution.py:39
  96.5 1.3 collective-permute-start
  97.8 7.0 %psum.23 = f32[1,2048]{1,0:T(1,128)} all-reduce(f32[1,2048]{1,0:T(1,128)S(1)} %bitcast.38), channel_id=1, replica_groups=mesh['dp'=4,'pipe'=2,'tensor'=4] {'dp'}, use_global_device_ids=true, to_apply=%region_6.0 | all-reduce | flops 2048 | bytes 16384 | tf_op jit(solution)/shard_map/psum | solution.py:44
  104.8 39.9 %collective-permute-done = bf16[512,2048]{1,0:T(8,128)(2,1)S(1)} collective-permute-done((bf16[512,2048]{1,0:T(8,128)(2,1)}, bf16[512,2048]{1,0:T(8,128)(2,1)S(1)}, u32[]{:S(2)}, u32[]{:S(2)}) %collective-permute-start) | collective-permute-done | bytes 2097184 | tf_op jit(solution)/shard_map/ppermute | solution.py:12
  144.7 0.0 reduce-scatter.2.cloned.1.call-done
  144.7 1.3 copy.9
  (2 shorter events, 0.0 us)
Async XLA Ops:
  7.2 51.1 %all-gather.3.cloned.1.call-start = ((), (), s32[]{:S(2)}) async-start(), calls=%async_computation.2 | async-start | bytes 2621440 | tf_op jit(solution)/shard_map/all_gather | solution.py:27
  7.9 136.8 %reduce-scatter.2.cloned.1.call-start = ((), (), s32[]{:S(2)}) async-start(), calls=%async_computation.1 | async-start | bytes 10485760 | tf_op jit(solution)/shard_map/reduce_scatter | solution.py:45
  68.4 1.6 %copy-start = (bf16[1,1,512,2048]{3,2,1,0:T(8,128)(2,1)S(1)}, bf16[1,1,512,2048]{3,2,1,0:T(8,128)(2,1)}, u32[]{:S(2)}) copy-start(bf16[1,1,512,2048]{3,2,1,0:T(8,128)(2,1)} %param.5) | copy-start | bytes 6291460
  96.5 48.2 %collective-permute-start = (bf16[512,2048]{1,0:T(8,128)(2,1)}, bf16[512,2048]{1,0:T(8,128)(2,1)S(1)}, u32[]{:S(2)}, u32[]{:S(2)}) collective-permute-start(bf16[512,2048]{1,0:T(8,128)(2,1)} %fusion.10), channel_id=1, source_target_pairs={{4,0},{5,1},{6,2},{7,3},{12,8},{13,9},{14,10},{15,11},{20,16},{21,... | collective-permute-start | bytes 6291464 | tf_op jit(solution)/shard_map/ppermute | solution.py:12
Sparse Core Ops, SparseCore 0:
  9.6 48.6 all-gather.2
  68.5 70.6 reduce-scatter.1
where the time goes:
time: 153 us
  waiting for transfers between devices  74.5 us (49%)
  blocking collectives  29.6 us (19%)
  matrix products  21.9 us (14%)
  between operations  14.1 us (9%)
  other arithmetic  8.53 us (6%)
  local copies, waits for them, and re-layouts  2.89 us (2%)
    ppermute x1, waiting for transfers between devices, from_behind(): return lax.ppermute(block, axis, route)  39.9 us
    all_gather x1, waiting for transfers between devices, on_device(): piece = lax.all_gather(grad_kv, 'tensor', axis=1, tiled=True)  33.9 us
    psum x1, blocking collectives, on_device(): total_squares = lax.psum(local_squares, 'tensor')  13.7 us
    dot_general x1, matrix products, on_device(): lax.dot_general(piece, weight, (((1,), (1,)), ((), ())), preferred_elemen...  11.8 us
    dot_general x1, matrix products, on_device(): lax.dot_general(hidden, piece, (((0,), (0,)), ((), ())), preferred_elemen...  10.1 us
    psum x1, blocking collectives, on_device(): mean_term = lax.psum(local_dot, 'tensor') / D  8.96 us
    psum x1, blocking collectives, on_device(): gain_total = lax.psum(gain_part, 'dp')  7.03 us
    convert_element_type x1, other arithmetic, on_device(): (grad_out.astype(jnp.float32) + rstd * (scaled - normed * mean_term)).ast...  5.73 us
  transfers between devices with their start and end apart: 3, of which 2 were waited for; matrix products, arithmetic and copies ran while one was open for 13% of the time, Pallas kernels for 0%

commit v1 on v0

--- a/solution.py
+++ b/solution.py
@@ -20,7 +20,12 @@
     weight = kv_weight[0]
     values = rows.astype(jnp.float32)
     local_squares = jnp.sum(values * values, axis=1, keepdims=True)
-    total_squares = lax.psum(local_squares, "tensor")
+
+    def _touch_wires(s0, comm_axis):
+        later = lax.all_gather(s0, comm_axis)
+        return jnp.sum(later, 0)
+
+    total_squares = _touch_wires(local_squares, comm_axis="tensor")
     rstd = lax.rsqrt(total_squares / D + 1e-05)
     normed = values * rstd
     hidden = (normed * gain_f).astype(jnp.bfloat16)

time: 153 us -> 153 us (level)
    psum x1 -> x0, blocking collectives: 13.7 us -> none  [on_device(): total_squares = lax.psum(local_squares, 'tensor')]
    all_gather x0 -> x1, blocking collectives: none -> 13.6 us  [_touch_wires(): later = lax.all_gather(s0, comm_axis)]
where the time goes in v1:
time: 153 us
  waiting for transfers between devices  74.2 us (48%)
  blocking collectives  29.6 us (19%)
  matrix products  22 us (14%)
  between operations  14.1 us (9%)
  other arithmetic  8.68 us (6%)
  local copies, waits for them, and re-layouts  2.89 us (2%)
    ppermute x1, waiting for transfers between devices, from_behind(): return lax.ppermute(block, axis, route)  39.7 us
    all_gather x1, waiting for transfers between devices, on_device(): piece = lax.all_gather(grad_kv, 'tensor', axis=1, tiled=True)  33.8 us
    all_gather x1, blocking collectives, _touch_wires(): later = lax.all_gather(s0, comm_axis)  13.6 us
    dot_general x1, matrix products, on_device(): lax.dot_general(piece, weight, (((1,), (1,)), ((), ())), preferred_elemen...  11.8 us
    dot_general x1, matrix products, on_device(): lax.dot_general(hidden, piece, (((0,), (0,)), ((), ())), preferred_elemen...  10.1 us
    psum x1, blocking collectives, on_device(): mean_term = lax.psum(local_dot, 'tensor') / D  8.89 us
    psum x1, blocking collectives, on_device(): gain_total = lax.psum(gain_part, 'dp')  7.03 us
    convert_element_type x1, other arithmetic, on_device(): (grad_out.astype(jnp.float32) + rstd * (scaled - normed * mean_term)).ast...  5.86 us
  transfers between devices with their start and end apart: 3, of which 2 were waited for; matrix products, arithmetic and copies ran while one was open for 13% of the time, Pallas kernels for 0%

profile of v1, /device:TPU:0, one launch (start us, length us, event | category | flops | bytes accessed | tf_op | source)
XLA Modules:
  0.0 152.7 jit_solution(17640072642552504765)
XLA Ops:
  7.2 0.0 all-gather.5.cloned.1.call-start
  7.2 0.7 all-gather.5.cloned.1.call-update
  7.9 0.0 reduce-scatter.2.cloned.1.call-start
  7.9 0.7 mul.66
  8.7 2.1 %fusion.13 = f32[512]{0:T(512)S(1)} fusion(bf16[1,1,512,2048]{3,2,1,0:T(8,128)(2,1)} %param.5), kind=kLoop, calls=%fused_computation.16 | loop fusion | flops 3145216 | bytes 2099200 | tf_op jit(solution)/shard_map/reduce_sum | solution.py:22
  10.7 13.6 %all-gather.2 = f32[4,1,512]{2,1,0:T(1,128)S(1)} all-gather(f32[1,1,512]{2,1,0:T(1,128)S(1)} %bitcast.36), channel_id=2, replica_groups=mesh['dp'=4,'pipe'=2,'tensor'=4] {'tensor'}, dimensions={0}, use_global_device_ids=true | all-gather | bytes 10240 | tf_op jit(solution)/shard_map/all_gather | solution.py:25
  24.4 33.8 %all-gather.5.cloned.1.call-done = bf16[1,1,512,2048]{3,2,1,0:T(8,128)(2,1)} async-done(((bf16[1,1,512,512]{3,2,1,0:T(8,128)(2,1)}), bf16[1,1,512,2048]{3,2,1,0:T(8,128)(2,1)}) %all-gather.5.cloned.1.call-update) | async-done | bytes 2097168 | tf_op jit(solution)/shard_map/all_gather | solution.py:32
  58.3 10.1 %convolution_convert_fusion = bf16[2048,2048]{1,0:T(8,128)(2,1)} fusion(bf16[1,1,512,2048]{3,2,1,0:T(8,128)(2,1)} %param.5, bf16[1,1,512,2048]{3,2,1,0:T(8,128)(2,1)} %all-gather.5.cloned.1.call-done, f32[2048]{0:T(1024)S(1)} %bitcast.33, f32[512]{0:T(512)S(1)} %add_rsqrt_fusion), kind=kOutput, calls=%fused_computation.2 | convolution fusion | flops 4303355904 | bytes 12593152 | tf_op jit(solution)/shard_map/dot_general | solution.py:36
  68.4 0.0 copy-start
  68.4 0.0 reduce-scatter.2.cloned.1.call-update
  68.4 1.6 %copy-done = bf16[1,1,512,2048]{3,2,1,0:T(8,128)(2,1)S(1)} copy-done((bf16[1,1,512,2048]{3,2,1,0:T(8,128)(2,1)S(1)}, bf16[1,1,512,2048]{3,2,1,0:T(8,128)(2,1)}, u32[]{:S(2)}) %copy-start) | copy-done | bytes 2097176
  70.0 11.8 %fusion.12 = (f32[2048]{0:T(1024)S(1)}, f32[512]{0:T(512)S(1)}, f32[512,2048]{1,0:T(8,128)}) fusion(bf16[1,1,512,2048]{3,2,1,0:T(8,128)(2,1)S(1)} %copy-done, f32[512]{0:T(512)S(1)} %add_rsqrt_fusion, f32[2048]{0:T(1024)S(1)} %bitcast.34, bf16[1,2048,2048]{2,1,0:T(8,128)(2,1)} %param.9, bf16[1,1,512,2048]{3,2,1,0:T(8,128)(2,1)} %all-gather.5.cloned.1.call-done), kind=kOutput, calls=%fused_computation.15 | convolution fusion | flops 4302304768 | bytes 16797696 | tf_op jit(solution)/shard_map/dot_general | solution.py:33
  81.8 8.9 %psum.14 = f32[512,1]{0,1:T(1,128)S(1)} all-reduce(f32[512,1]{0,1:T(1,128)S(1)} %bitcast.39), channel_id=1, replica_groups=mesh['dp'=4,'pipe'=2,'tensor'=4] {'tensor'}, use_global_device_ids=true, to_apply=%region_3.0 | all-reduce | flops 512 | bytes 4096 | tf_op jit(solution)/shard_map/psum | solution.py:43
  90.7 5.9 %fusion.10 = bf16[512,2048]{1,0:T(8,128)(2,1)} fusion(f32[512,2048]{1,0:T(8,128)} %get-tuple-element.5, bf16[1,1,512,2048]{3,2,1,0:T(8,128)(2,1)} %param.6, bf16[1,1,512,2048]{3,2,1,0:T(8,128)(2,1)S(1)} %copy-done, f32[512]{0:T(512)S(1)} %bitcast.38, f32[2048]{0:T(1024)S(1)} %bitcast.35, f32[512]{0:T(512)S(1)} %add_rsqrt_fusion), kind=kLoop, calls=%fused_computation.13 | loop fusion | flops 9437184 | bytes 10498048 | tf_op jit(solution)/shard_map/convert_element_type | solution.py:44
  96.6 1.3 collective-permute-start
  97.9 7.0 %psum.15 = f32[1,2048]{1,0:T(1,128)} all-reduce(f32[1,2048]{1,0:T(1,128)S(1)} %bitcast.37), channel_id=1, replica_groups=mesh['dp'=4,'pipe'=2,'tensor'=4] {'dp'}, use_global_device_ids=true, to_apply=%region_6.0 | all-reduce | flops 2048 | bytes 16384 | tf_op jit(solution)/shard_map/psum | solution.py:49
  104.9 39.7 %collective-permute-done = bf16[512,2048]{1,0:T(8,128)(2,1)S(1)} collective-permute-done((bf16[512,2048]{1,0:T(8,128)(2,1)}, bf16[512,2048]{1,0:T(8,128)(2,1)S(1)}, u32[]{:S(2)}, u32[]{:S(2)}) %collective-permute-start) | collective-permute-done | bytes 2097184 | tf_op jit(solution)/shard_map/ppermute | solution.py:12
  144.6 0.0 reduce-scatter.2.cloned.1.call-done
  144.6 1.3 copy.9
  (3 shorter events, 0.0 us)
Async XLA Ops:
  7.2 51.1 %all-gather.5.cloned.1.call-start = ((), (), s32[]{:S(2)}) async-start(), calls=%async_computation.2 | async-start | bytes 2621440 | tf_op jit(solution)/shard_map/all_gather | solution.py:32
  7.9 136.7 %reduce-scatter.2.cloned.1.call-start = ((), (), s32[]{:S(2)}) async-start(), calls=%async_computation.1 | async-start | bytes 10485760 | tf_op jit(solution)/shard_map/reduce_scatter | solution.py:50
  68.4 1.6 %copy-start = (bf16[1,1,512,2048]{3,2,1,0:T(8,128)(2,1)S(1)}, bf16[1,1,512,2048]{3,2,1,0:T(8,128)(2,1)}, u32[]{:S(2)}) copy-start(bf16[1,1,512,2048]{3,2,1,0:T(8,128)(2,1)} %param.5) | copy-start | bytes 6291460
  96.6 48.0 %collective-permute-start = (bf16[512,2048]{1,0:T(8,128)(2,1)}, bf16[512,2048]{1,0:T(8,128)(2,1)S(1)}, u32[]{:S(2)}, u32[]{:S(2)}) collective-permute-start(bf16[512,2048]{1,0:T(8,128)(2,1)} %fusion.10), channel_id=1, source_target_pairs={{4,0},{5,1},{6,2},{7,3},{12,8},{13,9},{14,10},{15,11},{20,16},{21,... | collective-permute-start | bytes 6291464 | tf_op jit(solution)/shard_map/ppermute | solution.py:12
Sparse Core Ops, SparseCore 0:
  9.6 48.6 all-gather.4
  68.5 70.9 reduce-scatter.1
